TPU v7x, 32 devices: a whole 2x2x4 slice. The times are simulated.
32 devices in a mesh: rep: 2 (over x), member: 4 (over y, core), tp: 4 (over z).
Axes of the slice: x: 2, y: 2, z: 4, core: 2. Of those that a mesh axis runs over, the one named last changes fastest.
Arguments:
- states: bfloat16 [4096, 1024], P(('rep', 'member', 'tp')), parts along dimension 0, may hold values from -6 to 6
- member_of: int32 [4096, 1], P(('rep', 'member', 'tp')), parts along dimension 0, may hold values from 0 to 1; in each aligned block of 128 rows (0 to 127, 128 to 255, ...) at most 128 rows name the same one
- place: int32 [4096], P(('rep', 'member', 'tp')), parts along dimension 0, may hold values from 0 to 2047, as said below
- norm_gain: float32 [2, 1024], replicated, may hold values from 0.5 to 2
- w_up: bfloat16 [4, 1024, 2048], P('member', None, 'tp'), may hold values from -0.1875 to 0.1875
- w_down: bfloat16 [4, 2048, 1024], P('member', 'tp'), may hold values from -0.09375 to 0.09375
- policy_gain: float32 [1024], replicated, may hold values from 0.5 to 2
- w_policy: bfloat16 [1024, 128], replicated, may hold values from -0.1875 to 0.1875
Outputs:
- imagined: bfloat16 [4096, 1024], P(('rep', 'member', 'tp')), parts along dimension 0
- action: bfloat16 [4096, 128], P(('rep', 'member', 'tp')), parts along dimension 0
There are 2 independent parts, one for each index of `rep`. A program takes and returns all parts, laid end to end along the dimension named above; an argument that names none is the same for every part. Nothing has to cross between parts.
Inputs may be any that keep to these rules, and one draw needn't show every extreme that they name: `member_of`: at most 128 of the rows of one device name any one member, and that count is reached on some device. `place`: A permutation of the 2048 learner positions; learner device k holds positions k * 128 to (k + 1) * 128 - 1, and the rows of each device go exactly 8 to every learner device.
All inputs are finite; a program needn't handle non-finite values.
Results may differ from a plain program's by a relative error of at most 0.0069.
Values may be sent and summed in bfloat16 or wider, within the bound.
No kernel may reach another device: no remote copies, remote signals or barrier semaphores. Data moves between devices by JAX's collectives and lax.ppermute only.
A program may use at most 128 MiB of HBM per device.

v0:
```python
import jax
import jax.numpy as jnp
from jax import lax
from jax.sharding import PartitionSpec as P


def from_partner(value, axis, distance):
    return lax.ppermute(value, axis, [(i, i ^ 1 << distance) for i in range(lax.axis_size(axis))])


def rms_scale(values, gain):
    mean_square = jnp.mean(values * values, axis=-1, keepdims=True)
    return values * lax.rsqrt(mean_square + 1e-06) * gain


def running_rank(member_hits):
    return jnp.sum((jnp.cumsum(member_hits, axis=0) - member_hits) * member_hits, axis=1)


def local(states, member_of, place, norm_gain, w_up, w_down, policy_gain, w_policy):
    n_member = lax.axis_size("member")
    n_tp = lax.axis_size("tp")
    n_dev = n_member * n_tp
    group_width = 2 * n_tp
    member_total = n_member // 2
    rows_here = states.shape[0]
    feature_width = states.shape[1]
    slot_count = 2 * rows_here // n_dev
    member = member_of[:, 0]
    member_hits = (member[:, None] == jnp.arange(member_total, dtype=jnp.int32)[None, :]).astype(
        jnp.int32
    )
    earlier = running_rank(member_hits)
    target = (member * group_width + earlier % group_width) * slot_count + earlier // group_width
    picker = (jnp.arange(n_dev * slot_count, dtype=jnp.int32)[:, None] == target[None, :]).astype(
        jnp.bfloat16
    )
    outgoing = jnp.dot(picker, states, preferred_element_type=jnp.float32).astype(jnp.bfloat16)
    arrived = lax.all_to_all(
        outgoing.reshape(n_dev, slot_count, feature_width),
        ("member", "tp"),
        split_axis=0,
        concat_axis=0,
        tiled=True,
    )
    arrived = arrived.reshape(n_dev * slot_count, feature_width)
    own_member = lax.axis_index("member") // 2
    gain_here = lax.dynamic_index_in_dim(norm_gain, own_member, 0, keepdims=False)
    normed = rms_scale(arrived.astype(jnp.float32), gain_here).astype(jnp.bfloat16)
    up_local = jnp.concatenate([w_up[0], from_partner(w_up[0], "member", 0)], axis=1)
    down_local = jnp.concatenate([w_down[0], from_partner(w_down[0], "member", 0)], axis=0)
    hidden = jax.nn.gelu(
        jnp.dot(
            lax.all_gather(normed, "tp", axis=0, tiled=True),
            up_local,
            preferred_element_type=jnp.float32,
        )
    ).astype(jnp.bfloat16)
    change = lax.psum_scatter(
        jnp.dot(hidden, down_local, preferred_element_type=jnp.float32),
        "tp",
        scatter_dimension=0,
        tiled=True,
    )
    predicted = (arrived.astype(jnp.float32) + change).astype(jnp.bfloat16)
    returned = lax.all_to_all(
        predicted.reshape(n_dev, slot_count, feature_width),
        ("member", "tp"),
        split_axis=0,
        concat_axis=0,
        tiled=True,
    )
    returned = returned.reshape(n_dev * slot_count, feature_width)
    own_rows = jnp.einsum("sr,sd->rd", picker, returned, preferred_element_type=jnp.float32).astype(
        jnp.bfloat16
    )
    per_learner = rows_here // n_dev
    learner = place // rows_here
    spot_index = place % rows_here
    learner_hits = (learner[:, None] == jnp.arange(n_dev, dtype=jnp.int32)[None, :]).astype(
        jnp.int32
    )
    lane_index = learner * per_learner + running_rank(learner_hits)
    placer = jnp.arange(rows_here, dtype=jnp.int32)[:, None] == lane_index[None, :]
    packed = jnp.dot(
        placer.astype(jnp.bfloat16), own_rows, preferred_element_type=jnp.float32
    ).astype(jnp.bfloat16)
    packed_spot = jnp.sum(placer.astype(jnp.int32) * spot_index[None, :], axis=1)
    arrivals, arrival_spots = (
        lax.all_to_all(
            packed.reshape(n_dev, per_learner, feature_width),
            ("member", "tp"),
            split_axis=0,
            concat_axis=0,
            tiled=True,
        ),
        lax.all_to_all(
            packed_spot.reshape(n_dev, per_learner),
            ("member", "tp"),
            split_axis=0,
            concat_axis=0,
            tiled=True,
        ),
    )
    arrivals = arrivals.reshape(rows_here, feature_width)
    arrival_spots = arrival_spots.reshape(rows_here)
    settle = (jnp.arange(rows_here, dtype=jnp.int32)[:, None] == arrival_spots[None, :]).astype(
        jnp.bfloat16
    )
    imagined = jnp.dot(settle, arrivals, preferred_element_type=jnp.float32).astype(jnp.bfloat16)
    policy_normed = rms_scale(imagined.astype(jnp.float32), policy_gain).astype(jnp.bfloat16)
    action = jnp.tanh(jnp.dot(policy_normed, w_policy, preferred_element_type=jnp.float32)).astype(
        jnp.bfloat16
    )
    return (imagined, action)


def solution(mesh):
    in_specs = (
        P(("rep", "member", "tp"), None),
        P(("rep", "member", "tp"), None),
        P(("rep", "member", "tp")),
        P(),
        P("member", None, "tp"),
        P("member", "tp", None),
        P(),
        P(),
    )
    out_specs = (P(("rep", "member", "tp"), None), P(("rep", "member", "tp"), None))
    return jax.shard_map(local, mesh=mesh, in_specs=in_specs, out_specs=out_specs, check_vma=False)
```

profile of v0, /device:TPU:0, one launch (start us, length us, event | category | flops | bytes accessed | tf_op | source)
XLA Modules:
  0.0 218.8 jit_solution(4283796861576501177)
XLA Ops:
  7.2 0.9 fusion.41
  8.3 0.8 select_reduce_fusion
  9.1 0.7 multiply_add_fusion
  9.8 1.1 convolution_convert_fusion
  10.9 7.4 %all-to-all-start.1 = ((bf16[16,16,1024]{2,1,0:T(8,128)(2,1)}), bf16[16,16,1024]{2,1,0:T(8,128)(2,1)S(1)}, u32[]{:S(2)}, u32[]{:S(2)}) async-start(bf16[16,16,1024]{2,1,0:T(8,128)(2,1)} %bitcast.2), calls=%async_computation.1 | async-start | bytes 1048576 | tf_op jit(solution)/shard_map/all_to_all | solution.py:39
  18.3 0.7 constant_dynamic-slice_fusion
  19.0 14.9 %all-to-all-done.1 = bf16[16,16,1024]{2,1,0:T(8,128)(2,1)S(1)} async-done(((bf16[16,16,1024]{2,1,0:T(8,128)(2,1)}), bf16[16,16,1024]{2,1,0:T(8,128)(2,1)S(1)}, u32[]{:S(2)}, u32[]{:S(2)}) %all-to-all-start.1) | async-done | bytes 524320 | tf_op jit(solution)/shard_map/all_to_all | solution.py:39
  34.2 1.0 fusion.29
  35.9 2.8 %collective-permute-done = bf16[1024,512]{1,0:T(8,128)(2,1)S(1)} collective-permute-done((bf16[1024,512]{1,0:T(8,128)(2,1)S(1)}, bf16[1024,512]{1,0:T(8,128)(2,1)S(1)}, u32[]{:S(2)}, u32[]{:S(2)}) %collective-permute-start) | collective-permute-done | bytes 1048608 | tf_op jit(solution)/shard_map/ppermute | solution.py:8
  38.6 1.0 copy-done.4
  39.6 40.4 %all-gather.2.cloned.1.call-done = bf16[1024,1024]{1,0:T(8,128)(2,1)} async-done(((bf16[256,1024]{1,0:T(8,128)(2,1)}), bf16[1024,1024]{1,0:T(8,128)(2,1)}) %all-gather.2.cloned.1.call-update) | async-done | bytes 2097168 | tf_op jit(solution)/shard_map/all_gather | solution.py:54
  80.0 8.7 %fusion.8 = f32[1024,1024]{1,0:T(8,128)} fusion(bf16[512,1024]{1,0:T(8,128)(2,1)} %collective-permute-done.1, bf16[512,1024]{1,0:T(8,128)(2,1)S(1)} %bitcast.34, bf16[1024,1024]{1,0:T(8,128)(2,1)} %all-gather.2.cloned.1.call-done, bf16[1024,512]{1,0:T(8,128)(2,1)} %copy-done.4, bf16[1024,512]{1,0:T(8,128)(2,1)S(1)} %bitcast.36), kind=kOutput, calls=%fused_computation.9 | convolution fusion | flops 4312793088 | bytes 10485760 | tf_op jit(solution)/shard_map/dot_general | solution.py:60
  88.7 75.6 %reduce-scatter.2.cloned.1.call-done = f32[256,1024]{1,0:T(8,128)} async-done(((f32[1024,1024]{1,0:T(8,128)}), f32[256,1024]{1,0:T(8,128)}) %reduce-scatter.2.cloned.1.call-update) | async-done | bytes 1048592 | tf_op jit(solution)/shard_map/reduce_scatter | solution.py:59
  164.4 2.2 fusion.30
  166.5 5.2 %all-to-all-start.2 = ((bf16[16,16,1024]{2,1,0:T(8,128)(2,1)}), bf16[16,16,1024]{2,1,0:T(8,128)(2,1)S(1)}, u32[]{:S(2)}, u32[]{:S(2)}) async-start(bf16[16,16,1024]{2,1,0:T(8,128)(2,1)} %bitcast.7), calls=%async_computation.3 | async-start | bytes 1048576 | tf_op jit(solution)/shard_map/all_to_all | solution.py:66
  172.4 0.7 all_to_all.15
  173.1 14.4 %all-to-all-done.2 = bf16[16,16,1024]{2,1,0:T(8,128)(2,1)S(1)} async-done(((bf16[16,16,1024]{2,1,0:T(8,128)(2,1)}), bf16[16,16,1024]{2,1,0:T(8,128)(2,1)S(1)}, u32[]{:S(2)}, u32[]{:S(2)}) %all-to-all-start.2) | async-done | bytes 524320 | tf_op jit(solution)/shard_map/all_to_all | solution.py:66
  187.5 3.5 %all-to-all-start = ((s32[16,1,8]{2,1,0:T(1,128)}), s32[16,1,8]{2,1,0:T(1,128)S(1)}, u32[]{:S(2)}, u32[]{:S(2)}) async-start(s32[16,1,8]{2,1,0:T(1,128)} %bitcast), calls=%async_computation | async-start | bytes 16384 | tf_op jit(solution)/shard_map/all_to_all | solution.py:97
  190.9 1.2 fusion.25
  192.1 5.1 %all-to-all-done = s32[16,1,8]{2,1,0:T(1,128)S(1)} async-done(((s32[16,1,8]{2,1,0:T(1,128)}), s32[16,1,8]{2,1,0:T(1,128)S(1)}, u32[]{:S(2)}, u32[]{:S(2)}) %all-to-all-start) | async-done | bytes 544 | tf_op jit(solution)/shard_map/all_to_all | solution.py:97
  197.2 3.5 %all-to-all-start.3 = ((bf16[16,8,1024]{2,1,0:T(8,128)(2,1)}), bf16[16,8,1024]{2,1,0:T(8,128)(2,1)S(1)}, u32[]{:S(2)}, u32[]{:S(2)}) async-start(bf16[16,8,1024]{2,1,0:T(8,128)(2,1)} %fusion.25), calls=%async_computation.4 | async-start | bytes 524288 | tf_op jit(solution)/shard_map/all_to_all | solution.py:90
  201.2 0.7 reduce.4
  202.0 8.7 %all-to-all-done.3 = bf16[16,8,1024]{2,1,0:T(8,128)(2,1)S(1)} async-done(((bf16[16,8,1024]{2,1,0:T(8,128)(2,1)}), bf16[16,8,1024]{2,1,0:T(8,128)(2,1)S(1)}, u32[]{:S(2)}, u32[]{:S(2)}) %all-to-all-start.3) | async-done | bytes 262176 | tf_op jit(solution)/shard_map/all_to_all | solution.py:90
  211.1 0.9 fusion.26
  (36 shorter events, 2.7 us)
Async XLA Ops:
  7.2 2.6 %copy-start = (bf16[128,1024]{1,0:T(8,128)(2,1)S(1)}, bf16[128,1024]{1,0:T(8,128)(2,1)}, u32[]{:S(2)}) copy-start(bf16[128,1024]{1,0:T(8,128)(2,1)} %param.8) | copy-start | bytes 786436
  7.2 28.1 %copy-start.3 = (bf16[1,1024,512]{2,1,0:T(8,128)(2,1)S(1)}, bf16[1,1024,512]{2,1,0:T(8,128)(2,1)}, u32[]{:S(2)}) copy-start(bf16[1,1024,512]{2,1,0:T(8,128)(2,1)} %param.12) | copy-start | bytes 3145732
  7.2 28.2 %copy-start.2 = (bf16[1,512,1024]{2,1,0:T(8,128)(2,1)S(1)}, bf16[1,512,1024]{2,1,0:T(8,128)(2,1)}, u32[]{:S(2)}) copy-start(bf16[1,512,1024]{2,1,0:T(8,128)(2,1)} %param.13) | copy-start | bytes 3145732
  10.9 23.1 %all-to-all-start.1 = ((bf16[16,16,1024]{2,1,0:T(8,128)(2,1)}), bf16[16,16,1024]{2,1,0:T(8,128)(2,1)S(1)}, u32[]{:S(2)}, u32[]{:S(2)}) async-start(bf16[16,16,1024]{2,1,0:T(8,128)(2,1)} %bitcast.2), calls=%async_computation.1 | async-start | bytes 1048576 | tf_op jit(solution)/shard_map/all_to_all | solution.py:39
  18.3 61.7 %all-gather.2.cloned.1.call-start = ((), (), s32[]{:S(2)}) async-start(), calls=%async_computation.5 | async-start | bytes 2621440 | tf_op jit(solution)/shard_map/all_gather | solution.py:54
  35.2 129.1 %reduce-scatter.2.cloned.1.call-start = ((), (), s32[]{:S(2)}) async-start(), calls=%async_computation.6 | async-start | bytes 5242880 | tf_op jit(solution)/shard_map/reduce_scatter | solution.py:59
  35.3 3.3 %collective-permute-start = (bf16[1024,512]{1,0:T(8,128)(2,1)S(1)}, bf16[1024,512]{1,0:T(8,128)(2,1)S(1)}, u32[]{:S(2)}, u32[]{:S(2)}) collective-permute-start(bf16[1024,512]{1,0:T(8,128)(2,1)S(1)} %bitcast.35), channel_id=1, source_target_pairs={{0,4},{4,0},{8,12},{12,8},{1,5},{5,1},{9,13},{13,9},{2,6},{6,2},{1... | collective-permute-start | bytes 3145736 | tf_op jit(solution)/shard_map/ppermute | solution.py:8
  35.4 4.3 %collective-permute-start.1 = (bf16[512,1024]{1,0:T(8,128)(2,1)S(1)}, bf16[512,1024]{1,0:T(8,128)(2,1)}, u32[]{:S(2)}, u32[]{:S(2)}) collective-permute-start(bf16[512,1024]{1,0:T(8,128)(2,1)S(1)} %bitcast.33), channel_id=1, source_target_pairs={{0,4},{4,0},{8,12},{12,8},{1,5},{5,1},{9,13},{13,9},{2,6},{6,2},{1... | collective-permute-start | bytes 3145736 | tf_op jit(solution)/shard_map/ppermute | solution.py:8
  38.6 1.0 copy-start.4
  88.7 83.1 %copy-start.7 = (s32[128]{0:T(128)S(1)}, s32[128]{0:T(128)}, u32[]{:S(2)}) copy-start(s32[128]{0:T(128)} %param.10) | copy-start | bytes 1540
  88.7 122.4 %copy-start.5 = (bf16[1024,128]{1,0:T(8,128)(2,1)S(1)}, bf16[1024,128]{1,0:T(8,128)(2,1)}, u32[]{:S(2)}) copy-start(bf16[1024,128]{1,0:T(8,128)(2,1)} %param.15) | copy-start | bytes 786436
  88.7 122.4 %copy-start.6 = (f32[1024]{0:T(1024)S(1)}, f32[1024]{0:T(1024)}, u32[]{:S(2)}) copy-start(f32[1024]{0:T(1024)} %param.14) | copy-start | bytes 12292
  166.5 20.9 %all-to-all-start.2 = ((bf16[16,16,1024]{2,1,0:T(8,128)(2,1)}), bf16[16,16,1024]{2,1,0:T(8,128)(2,1)S(1)}, u32[]{:S(2)}, u32[]{:S(2)}) async-start(bf16[16,16,1024]{2,1,0:T(8,128)(2,1)} %bitcast.7), calls=%async_computation.3 | async-start | bytes 1048576 | tf_op jit(solution)/shard_map/all_to_all | solution.py:66
  187.5 9.7 %all-to-all-start = ((s32[16,1,8]{2,1,0:T(1,128)}), s32[16,1,8]{2,1,0:T(1,128)S(1)}, u32[]{:S(2)}, u32[]{:S(2)}) async-start(s32[16,1,8]{2,1,0:T(1,128)} %bitcast), calls=%async_computation | async-start | bytes 16384 | tf_op jit(solution)/shard_map/all_to_all | solution.py:97
  197.2 13.6 %all-to-all-start.3 = ((bf16[16,8,1024]{2,1,0:T(8,128)(2,1)}), bf16[16,8,1024]{2,1,0:T(8,128)(2,1)S(1)}, u32[]{:S(2)}, u32[]{:S(2)}) async-start(bf16[16,8,1024]{2,1,0:T(8,128)(2,1)} %fusion.25), calls=%async_computation.4 | async-start | bytes 524288 | tf_op jit(solution)/shard_map/all_to_all | solution.py:90
  211.0 1.0 copy-start.1
Sparse Core Ops, SparseCore 0:
  35.4 44.6 all-gather.1
  88.9 75.4 reduce-scatter.1
where the time goes:
time: 219 us
  waiting for transfers between devices  162 us (74%)
  starting transfers between devices  20.2 us (9%)
  between operations  14.2 us (6%)
  matrix products  12.2 us (6%)
  other arithmetic  7.14 us (3%)
  local copies, waits for them, and re-layouts  3.1 us (1%)
    reduce_scatter x1, waiting for transfers between devices, local(): lax.psum_scatter(jnp.dot(hidden, down_local, preferred_element_type=jnp.f...  75.6 us
    all_gather x1, waiting for transfers between devices, local(): lax.all_gather(normed, 'tp', axis=0, tiled=True)  40.4 us
    all_to_all x1, waiting for transfers between devices, local(): lax.all_to_all(outgoing.reshape(n_dev, slot_count, feature_width), ('memb...  14.9 us
    all_to_all x1, waiting for transfers between devices, local(): lax.all_to_all(predicted.reshape(n_dev, slot_count, feature_width), ('mem...  14.4 us
    all_to_all x1, waiting for transfers between devices, local(): lax.all_to_all(packed.reshape(n_dev, per_learner, feature_width), ('membe...  8.74 us
    dot_general x1, matrix products, local(): jnp.dot(hidden, down_local, preferred_element_type=jnp.float32)  8.7 us
    all_to_all x1, starting transfers between devices, local(): lax.all_to_all(outgoing.reshape(n_dev, slot_count, feature_width), ('memb...  7.39 us
    all_to_all x1, starting transfers between devices, local(): lax.all_to_all(predicted.reshape(n_dev, slot_count, feature_width), ('mem...  5.21 us
  transfers between devices with their start and end apart: 8, of which 7 were waited for; matrix products, arithmetic and copies ran while one was open for 2% of the time, Pallas kernels for 0%

commit v1 on v0

--- a/solution.py
+++ b/solution.py
@@ -1,7 +1,46 @@
+import functools
 import jax
 import jax.numpy as jnp
 from jax import lax
 from jax.sharding import PartitionSpec as P
+
+
+def serve_zone(xs, peer_axis, where_dim):
+    m_next = jax.lax.axis_size(peer_axis)
+    latest, known, passed = (m_next, jax.lax.axis_index(peer_axis), xs.shape[where_dim])
+    blocks_here = []
+    for j, nth in enumerate(xs.shape):
+        blocks_here.append(nth * latest if j == where_dim else nth)
+    aux = lax.dynamic_update_slice_in_dim(
+        jnp.zeros(blocks_here, xs.dtype), xs, known * passed, axis=where_dim
+    )
+    back = block_now = xs
+    src_i = 1
+    while src_i < latest // 2 + 1:
+        slots = []
+        j = 0
+        while j < latest:
+            slots.append((j, (j + 1) % latest))
+            j += 1
+        back = jax.lax.ppermute(back, axis_name=peer_axis, perm=slots)
+        aux = lax.dynamic_update_slice_in_dim(
+            aux, back, (known - src_i) % latest * passed, axis=where_dim
+        )
+        if 2 * src_i < latest:
+            views = []
+            j = 0
+            while j < latest:
+                views.append((j, (j - 1) % latest))
+                j += 1
+            block_now = jax.lax.ppermute(block_now, axis_name=peer_axis, perm=views)
+            aux = lax.dynamic_update_slice_in_dim(
+                aux, block_now, (known + src_i) % latest * passed, axis=where_dim
+            )
+        src_i += 1
+    return aux
+
+
+match_cards_on = functools.partial(serve_zone, peer_axis="tp", where_dim=0)
 
 
 def from_partner(value, axis, distance):
@@ -50,11 +89,7 @@
     up_local = jnp.concatenate([w_up[0], from_partner(w_up[0], "member", 0)], axis=1)
     down_local = jnp.concatenate([w_down[0], from_partner(w_down[0], "member", 0)], axis=0)
     hidden = jax.nn.gelu(
-        jnp.dot(
-            lax.all_gather(normed, "tp", axis=0, tiled=True),
-            up_local,
-            preferred_element_type=jnp.float32,
-        )
+        jnp.dot(match_cards_on(normed), up_local, preferred_element_type=jnp.float32)
     ).astype(jnp.bfloat16)
     change = lax.psum_scatter(
         jnp.dot(hidden, down_local, preferred_element_type=jnp.float32),

time: 219 us -> 212 us (0.968)
  waiting for transfers between devices: 162 us -> 150 us
  starting transfers between devices: 20.2 us -> 24.2 us
    all_gather x1 -> x0, waiting for transfers between devices: 40.4 us -> none  [local(): lax.all_gather(normed, 'tp', axis=0, tiled=True)]
    ppermute x0 -> x3, waiting for transfers between devices: none -> 31.4 us  [the longest x2 23 us: serve_zone(): back = jax.lax.ppermute(back, axis_name=peer_axis, perm=slots)]
    ppermute x0 -> x3, starting transfers between devices: none -> 3.81 us  [the longest x1 3.74 us: serve_zone(): block_now = jax.lax.ppermute(block_now, axis_name=peer_axis, perm=views)]
    dynamic_update_slice x0 -> x3, local copies, waits for them, and re-layouts: none -> 3.26 us  [the longest x2 2.19 us: serve_zone(): lax.dynamic_update_slice_in_dim(aux, back, (known - src_i) % latest * pas...]
    ppermute x2, waiting for transfers between devices: 2.8 us -> 0.01 us  [from_partner(): lax.ppermute(value, axis, [(i, i ^ 1 << distance) for i in range(lax.axis...]
  transfers between devices with their start and end apart: 8 -> 10, of which waited for: 7 -> 8; matrix products, arithmetic and copies ran while one was open for 2% -> 3% of each run, Pallas kernels for 0% -> 0%
where the time goes in v1:
time: 212 us
  waiting for transfers between devices  150 us (71%)
  starting transfers between devices  24.2 us (11%)
  between operations  14.3 us (7%)
  matrix products  12.1 us (6%)
  other arithmetic  6.24 us (3%)
  local copies, waits for them, and re-layouts  4.94 us (2%)
    reduce_scatter x1, waiting for transfers between devices, local(): lax.psum_scatter(jnp.dot(hidden, down_local, preferred_element_type=jnp.f...  74.8 us
    ppermute x2, waiting for transfers between devices, serve_zone(): back = jax.lax.ppermute(back, axis_name=peer_axis, perm=slots)  23 us
    all_to_all x1, waiting for transfers between devices, local(): lax.all_to_all(outgoing.reshape(n_dev, slot_count, feature_width), ('memb...  15.6 us
    all_to_all x1, waiting for transfers between devices, local(): lax.all_to_all(predicted.reshape(n_dev, slot_count, feature_width), ('mem...  14.4 us
    all_to_all x1, waiting for transfers between devices, local(): lax.all_to_all(packed.reshape(n_dev, per_learner, feature_width), ('membe...  8.74 us
    dot_general x1, matrix products, local(): jnp.dot(hidden, down_local, preferred_element_type=jnp.float32)  8.68 us
    ppermute x1, waiting for transfers between devices, serve_zone(): block_now = jax.lax.ppermute(block_now, axis_name=peer_axis, perm=views)  8.4 us
    all_to_all x1, starting transfers between devices, local(): lax.all_to_all(outgoing.reshape(n_dev, slot_count, feature_width), ('memb...  7.39 us
  transfers between devices with their start and end apart: 10, of which 8 were waited for; matrix products, arithmetic and copies ran while one was open for 3% of the time, Pallas kernels for 0%

profile of v1, /device:TPU:0, one launch (start us, length us, event | category | flops | bytes accessed | tf_op | source)
XLA Modules:
  0.0 211.8 jit_solution(2933221774789861390)
XLA Ops:
  7.2 0.8 fusion.41
  8.1 0.8 select_reduce_fusion
  9.7 1.1 convolution_convert_fusion
  10.8 7.4 %all-to-all-start.1 = ((bf16[16,16,1024]{2,1,0:T(8,128)(2,1)}), bf16[16,16,1024]{2,1,0:T(8,128)(2,1)S(1)}, u32[]{:S(2)}, u32[]{:S(2)}) async-start(bf16[16,16,1024]{2,1,0:T(8,128)(2,1)} %bitcast.2), calls=%async_computation.1 | async-start | bytes 1048576 | tf_op jit(solution)/shard_map/all_to_all | solution.py:78
  18.3 15.6 %all-to-all-done.1 = bf16[16,16,1024]{2,1,0:T(8,128)(2,1)S(1)} async-done(((bf16[16,16,1024]{2,1,0:T(8,128)(2,1)}), bf16[16,16,1024]{2,1,0:T(8,128)(2,1)S(1)}, u32[]{:S(2)}, u32[]{:S(2)}) %all-to-all-start.1) | async-done | bytes 524320 | tf_op jit(solution)/shard_map/all_to_all | solution.py:78
  35.2 3.7 %collective-permute-start.1 = (bf16[256,1024]{1,0:T(8,128)(2,1)S(1)}, bf16[256,1024]{1,0:T(8,128)(2,1)}, u32[]{:S(2)}, u32[]{:S(2)}) collective-permute-start(bf16[256,1024]{1,0:T(8,128)(2,1)S(1)} %get-tuple-element.5), channel_id=1, source_target_pairs={{0,3},{1,0},{2,1},{3,2},{4,7},{5,4},{6,5},{7,6},{8,11},{9,8},{10,9... | collective-permute-start | bytes 1572872 | tf_op jit(solution)/shard_map/ppermute | solution.py:35
  39.0 12.4 %collective-permute-done = bf16[256,1024]{1,0:T(8,128)(2,1)} collective-permute-done((bf16[256,1024]{1,0:T(8,128)(2,1)S(1)}, bf16[256,1024]{1,0:T(8,128)(2,1)}, u32[]{:S(2)}, u32[]{:S(2)}) %collective-permute-start) | collective-permute-done | bytes 524320 | tf_op jit(solution)/shard_map/ppermute | solution.py:25
  51.4 1.1 constant_dynamic-update-slice_fusion.1
  52.5 8.4 %collective-permute-done.1 = bf16[256,1024]{1,0:T(8,128)(2,1)} collective-permute-done((bf16[256,1024]{1,0:T(8,128)(2,1)S(1)}, bf16[256,1024]{1,0:T(8,128)(2,1)}, u32[]{:S(2)}, u32[]{:S(2)}) %collective-permute-start.1) | collective-permute-done | bytes 524320 | tf_op jit(solution)/shard_map/ppermute | solution.py:35
  60.9 1.1 constant_dynamic-update-slice_fusion
  62.0 10.6 %collective-permute-done.2 = bf16[256,1024]{1,0:T(8,128)(2,1)} collective-permute-done((bf16[256,1024]{1,0:T(8,128)(2,1)}, bf16[256,1024]{1,0:T(8,128)(2,1)}, u32[]{:S(2)}, u32[]{:S(2)}) %collective-permute-start.2) | collective-permute-done | bytes 524320 | tf_op jit(solution)/shard_map/ppermute | solution.py:25
  72.6 1.1 constant_dynamic-update-slice_fusion.3
  73.7 8.7 %fusion.8 = f32[1024,1024]{1,0:T(8,128)} fusion(bf16[512,1024]{1,0:T(8,128)(2,1)} %collective-permute-done.4, bf16[512,1024]{1,0:T(8,128)(2,1)} %bitcast.34, bf16[1024,1024]{1,0:T(8,128)(2,1)S(1)} %constant_dynamic-update-slice_fusion.3, bf16[1024,512]{1,0:T(8,128)(2,1)} %collective-permute-done.3, bf16[1024,512]{1,0:T(8,128)(2,1)} %bitcast.36), kind=kOutput, calls=%fused_computation.9 | convolution fusion | flops 4312793088 | bytes 10485760 | tf_op jit(solution)/shard_map/dot_general | solution.py:95
  82.4 74.8 %reduce-scatter.2.cloned.1.call-done = f32[256,1024]{1,0:T(8,128)} async-done(((f32[1024,1024]{1,0:T(8,128)}), f32[256,1024]{1,0:T(8,128)}) %reduce-scatter.2.cloned.1.call-update) | async-done | bytes 1048592 | tf_op jit(solution)/shard_map/reduce_scatter | solution.py:94
  157.2 2.2 %fusion.30 = bf16[256,1024]{1,0:T(8,128)(2,1)} fusion(f32[256,1024]{1,0:T(8,128)} %reduce-scatter.2.cloned.1.call-done, bf16[16,16,1024]{2,1,0:T(8,128)(2,1)S(1)} %all-to-all-done.1), kind=kLoop, calls=%fused_computation.34 | loop fusion | flops 786432 | bytes 2097152 | tf_op jit(solution)/shard_map/convert_element_type | solution.py:100
  159.4 5.4 %all-to-all-start.2 = ((bf16[16,16,1024]{2,1,0:T(8,128)(2,1)}), bf16[16,16,1024]{2,1,0:T(8,128)(2,1)S(1)}, u32[]{:S(2)}, u32[]{:S(2)}) async-start(bf16[16,16,1024]{2,1,0:T(8,128)(2,1)} %bitcast.7), calls=%async_computation.3 | async-start | bytes 1048576 | tf_op jit(solution)/shard_map/all_to_all | solution.py:101
  165.3 0.7 all_to_all.15
  166.0 14.4 %all-to-all-done.2 = bf16[16,16,1024]{2,1,0:T(8,128)(2,1)S(1)} async-done(((bf16[16,16,1024]{2,1,0:T(8,128)(2,1)}), bf16[16,16,1024]{2,1,0:T(8,128)(2,1)S(1)}, u32[]{:S(2)}, u32[]{:S(2)}) %all-to-all-start.2) | async-done | bytes 524320 | tf_op jit(solution)/shard_map/all_to_all | solution.py:101
  180.4 3.5 %all-to-all-start = ((s32[16,1,8]{2,1,0:T(1,128)}), s32[16,1,8]{2,1,0:T(1,128)S(1)}, u32[]{:S(2)}, u32[]{:S(2)}) async-start(s32[16,1,8]{2,1,0:T(1,128)} %bitcast), calls=%async_computation | async-start | bytes 16384 | tf_op jit(solution)/shard_map/all_to_all | solution.py:132
  183.9 1.1 fusion.25
  185.0 5.1 %all-to-all-done = s32[16,1,8]{2,1,0:T(1,128)S(1)} async-done(((s32[16,1,8]{2,1,0:T(1,128)}), s32[16,1,8]{2,1,0:T(1,128)S(1)}, u32[]{:S(2)}, u32[]{:S(2)}) %all-to-all-start) | async-done | bytes 544 | tf_op jit(solution)/shard_map/all_to_all | solution.py:132
  190.1 3.5 %all-to-all-start.3 = ((bf16[16,8,1024]{2,1,0:T(8,128)(2,1)}), bf16[16,8,1024]{2,1,0:T(8,128)(2,1)S(1)}, u32[]{:S(2)}, u32[]{:S(2)}) async-start(bf16[16,8,1024]{2,1,0:T(8,128)(2,1)} %fusion.25), calls=%async_computation.4 | async-start | bytes 524288 | tf_op jit(solution)/shard_map/all_to_all | solution.py:125
  194.9 8.7 %all-to-all-done.3 = bf16[16,8,1024]{2,1,0:T(8,128)(2,1)S(1)} async-done(((bf16[16,8,1024]{2,1,0:T(8,128)(2,1)}), bf16[16,8,1024]{2,1,0:T(8,128)(2,1)S(1)}, u32[]{:S(2)}, u32[]{:S(2)}) %all-to-all-start.3) | async-done | bytes 262176 | tf_op jit(solution)/shard_map/all_to_all | solution.py:125
  204.0 0.9 fusion.26
  (36 shorter events, 4.4 us)
Async XLA Ops:
  7.2 2.5 %copy-start = (bf16[128,1024]{1,0:T(8,128)(2,1)S(1)}, bf16[128,1024]{1,0:T(8,128)(2,1)}, u32[]{:S(2)}) copy-start(bf16[128,1024]{1,0:T(8,128)(2,1)} %param.8) | copy-start | bytes 786436
  7.2 11.0 %copy-start.2 = (f32[2,1024]{1,0:T(2,128)S(1)}, f32[2,1024]{1,0:T(2,128)}, u32[]{:S(2)}) copy-start(f32[2,1024]{1,0:T(2,128)} %param.11) | copy-start | bytes 24580
  10.8 23.1 %all-to-all-start.1 = ((bf16[16,16,1024]{2,1,0:T(8,128)(2,1)}), bf16[16,16,1024]{2,1,0:T(8,128)(2,1)S(1)}, u32[]{:S(2)}, u32[]{:S(2)}) async-start(bf16[16,16,1024]{2,1,0:T(8,128)(2,1)} %bitcast.2), calls=%async_computation.1 | async-start | bytes 1048576 | tf_op jit(solution)/shard_map/all_to_all | solution.py:78
  18.2 139.0 %reduce-scatter.2.cloned.1.call-start = ((), (), s32[]{:S(2)}) async-start(), calls=%async_computation.5 | async-start | bytes 5242880 | tf_op jit(solution)/shard_map/reduce_scatter | solution.py:94
  34.6 16.8 %collective-permute-start = (bf16[256,1024]{1,0:T(8,128)(2,1)S(1)}, bf16[256,1024]{1,0:T(8,128)(2,1)}, u32[]{:S(2)}, u32[]{:S(2)}) collective-permute-start(bf16[256,1024]{1,0:T(8,128)(2,1)S(1)} %get-tuple-element.5), channel_id=1, source_target_pairs={{0,1},{1,2},{2,3},{3,0},{4,5},{5,6},{6,7},{7,4},{8,9},{9,10},{10,1... | collective-permute-start | bytes 1572872 | tf_op jit(solution)/shard_map/ppermute | solution.py:25
  34.7 39.0 %collective-permute-start.3 = (bf16[1024,512]{1,0:T(8,128)(2,1)}, bf16[1024,512]{1,0:T(8,128)(2,1)}, u32[]{:S(2)}, u32[]{:S(2)}) collective-permute-start(bf16[1024,512]{1,0:T(8,128)(2,1)} %bitcast.35), channel_id=1, source_target_pairs={{0,4},{4,0},{8,12},{12,8},{1,5},{5,1},{9,13},{13,9},{2,6},{6,2},{1... | collective-permute-start | bytes 3145736 | tf_op jit(solution)/shard_map/ppermute | solution.py:47
  34.7 38.9 %collective-permute-start.4 = (bf16[512,1024]{1,0:T(8,128)(2,1)}, bf16[512,1024]{1,0:T(8,128)(2,1)}, u32[]{:S(2)}, u32[]{:S(2)}) collective-permute-start(bf16[512,1024]{1,0:T(8,128)(2,1)} %bitcast.33), channel_id=1, source_target_pairs={{0,4},{4,0},{8,12},{12,8},{1,5},{5,1},{9,13},{13,9},{2,6},{6,2},{1... | collective-permute-start | bytes 3145736 | tf_op jit(solution)/shard_map/ppermute | solution.py:47
  35.2 25.7 %collective-permute-start.1 = (bf16[256,1024]{1,0:T(8,128)(2,1)S(1)}, bf16[256,1024]{1,0:T(8,128)(2,1)}, u32[]{:S(2)}, u32[]{:S(2)}) collective-permute-start(bf16[256,1024]{1,0:T(8,128)(2,1)S(1)} %get-tuple-element.5), channel_id=1, source_target_pairs={{0,3},{1,0},{2,1},{3,2},{4,7},{5,4},{6,5},{7,6},{8,11},{9,8},{10,9... | collective-permute-start | bytes 1572872 | tf_op jit(solution)/shard_map/ppermute | solution.py:35
  51.4 21.2 %collective-permute-start.2 = (bf16[256,1024]{1,0:T(8,128)(2,1)}, bf16[256,1024]{1,0:T(8,128)(2,1)}, u32[]{:S(2)}, u32[]{:S(2)}) collective-permute-start(bf16[256,1024]{1,0:T(8,128)(2,1)} %collective-permute-done), channel_id=1, source_target_pairs={{0,1},{1,2},{2,3},{3,0},{4,5},{5,6},{6,7},{7,4},{8,9},{9,10},{10,1... | collective-permute-start | bytes 1572872 | tf_op jit(solution)/shard_map/ppermute | solution.py:25
  159.4 44.7 %copy-start.3 = (bf16[1024,128]{1,0:T(8,128)(2,1)S(1)}, bf16[1024,128]{1,0:T(8,128)(2,1)}, u32[]{:S(2)}) copy-start(bf16[1024,128]{1,0:T(8,128)(2,1)} %param.15) | copy-start | bytes 786436
  159.4 44.7 %copy-start.4 = (f32[1024]{0:T(1024)S(1)}, f32[1024]{0:T(1024)}, u32[]{:S(2)}) copy-start(f32[1024]{0:T(1024)} %param.14) | copy-start | bytes 12292
  159.4 21.1 %all-to-all-start.2 = ((bf16[16,16,1024]{2,1,0:T(8,128)(2,1)}), bf16[16,16,1024]{2,1,0:T(8,128)(2,1)S(1)}, u32[]{:S(2)}, u32[]{:S(2)}) async-start(bf16[16,16,1024]{2,1,0:T(8,128)(2,1)} %bitcast.7), calls=%async_computation.3 | async-start | bytes 1048576 | tf_op jit(solution)/shard_map/all_to_all | solution.py:101
  180.4 9.7 %all-to-all-start = ((s32[16,1,8]{2,1,0:T(1,128)}), s32[16,1,8]{2,1,0:T(1,128)S(1)}, u32[]{:S(2)}, u32[]{:S(2)}) async-start(s32[16,1,8]{2,1,0:T(1,128)} %bitcast), calls=%async_computation | async-start | bytes 16384 | tf_op jit(solution)/shard_map/all_to_all | solution.py:132
  190.1 13.6 %all-to-all-start.3 = ((bf16[16,8,1024]{2,1,0:T(8,128)(2,1)}), bf16[16,8,1024]{2,1,0:T(8,128)(2,1)S(1)}, u32[]{:S(2)}, u32[]{:S(2)}) async-start(bf16[16,8,1024]{2,1,0:T(8,128)(2,1)} %fusion.25), calls=%async_computation.4 | async-start | bytes 524288 | tf_op jit(solution)/shard_map/all_to_all | solution.py:125
  204.0 1.0 copy-start.1
Sparse Core Ops, SparseCore 0:
  82.5 74.6 reduce-scatter.1
